TPU v7x, 256 devices: a whole 4x4x8 slice. The times are simulated.
256 devices in a mesh: space: 32 (over y_lo, z, core), chan: 8 (over x, y_hi).
Axes of the slice: x: 4, y: 4 (y_hi: 2, y_lo: 2; y = y_hi * 2 + y_lo), z: 8, core: 2. Of those that a mesh axis runs over, the one named last changes fastest.
Arguments:
- inputs: bfloat16 [32, 256, 2048], P('space', 'chan'), may hold values from -6 to 6
- weights: bfloat16 [27, 256, 256], P(None, 'chan'), may hold values from -0.078125 to 0.078125
- cotangent: bfloat16 [32, 256, 2048], P('space', 'chan'), may hold values from -6 to 6
Outputs:
- output: bfloat16 [32, 256, 2048], P('space', 'chan')
- input_grad: bfloat16 [32, 256, 2048], P('space', 'chan')
- weight_grad: float32 [27, 256, 256], P(None, 'chan')
All inputs are finite; a program needn't handle non-finite values.
Results may differ from a plain program's by a relative error of at most 0.001.
Values may be sent and summed in bfloat16 or wider, within the bound.
No kernel may reach another device: no remote copies, remote signals or barrier semaphores. Data moves between devices by JAX's collectives and lax.ppermute only.
A program may use at most 192 MiB of HBM per device.

v0:
```python
import jax
import jax.numpy as jnp
from jax import lax
from jax.sharding import PartitionSpec as P

PLANE_ROWS = 32
ROW_CELLS = 64


def extended(block, sides, width):
    for axis, dim in sides:
        count = lax.axis_size(axis)
        forward = [(i, i + 1) for i in range(count - 1)]
        backward = [(target, source) for source, target in forward]
        low = lax.ppermute(
            lax.slice_in_dim(block, block.shape[dim] - width, None, axis=dim), axis, forward
        )
        high = lax.ppermute(lax.slice_in_dim(block, 0, width, axis=dim), axis, backward)
        block = jnp.concatenate([low, block, high], axis=dim)
    return block


def plane_shift(field, tap_row, tap_col):
    lead = field.shape[:-1]
    grid = field.reshape(lead + (PLANE_ROWS, ROW_CELLS))
    padded = jnp.pad(grid, [(0, 0)] * len(lead) + [(1, 1), (1, 1)])
    window = padded[..., tap_row : tap_row + PLANE_ROWS, tap_col : tap_col + ROW_CELLS]
    return window.reshape(lead + (PLANE_ROWS * ROW_CELLS,))


def stack_at(padded, tap_row, tap_col):
    planes = padded.shape[0] - 2
    moved = plane_shift(padded, tap_row, tap_col)
    return jnp.concatenate(
        [moved[tap_depth : tap_depth + planes] for tap_depth in range(3)], axis=1
    )


def tap_weights(taps, tap_row, tap_col):
    return jnp.concatenate(
        [taps[tap_depth * 9 + tap_row * 3 + tap_col] for tap_depth in range(3)], axis=0
    )


def convolve(padded, taps):
    total = None
    for tap_row in range(3):
        for tap_col in range(3):
            term = jnp.einsum(
                "dcp,co->dop",
                stack_at(padded, tap_row, tap_col),
                tap_weights(taps, tap_row, tap_col),
                preferred_element_type=jnp.float32,
            )
            total = term if total is None else total + term
    return total


def weight_terms(padded, cot_whole, channels):
    pieces = [None] * 27
    for tap_row in range(3):
        for tap_col in range(3):
            block = jnp.einsum(
                "dcp,dop->co",
                stack_at(padded, tap_row, tap_col),
                cot_whole,
                preferred_element_type=jnp.float32,
            )
            block = block.reshape(3, channels, cot_whole.shape[1])
            for tap_depth in range(3):
                pieces[tap_depth * 9 + tap_row * 3 + tap_col] = block[tap_depth]
    return jnp.stack(pieces, axis=0)


def local(inputs, weights, cotangent):
    padded = extended(inputs, (("space", 0),), 1)
    partial_out = convolve(padded, weights)
    output = lax.psum_scatter(partial_out, "chan", scatter_dimension=1, tiled=True).astype(
        jnp.bfloat16
    )
    gathered = lax.all_gather(cotangent, "chan", axis=1, tiled=True)
    cot_padded = extended(gathered, (("space", 0),), 1)
    cot_whole = cot_padded[1:-1]
    flipped = jnp.transpose(weights[::-1], (0, 2, 1))
    input_grad = convolve(cot_padded, flipped).astype(jnp.bfloat16)
    local_terms = weight_terms(padded, cot_whole, inputs.shape[1])
    weight_grad = lax.psum(local_terms, "space")
    return (output, input_grad, weight_grad)


def solution(mesh):
    placed = (P("space", "chan", None), P(None, "chan", None), P("space", "chan", None))
    return jax.shard_map(
        local,
        mesh=mesh,
        in_specs=placed,
        out_specs=(P("space", "chan", None), P("space", "chan", None), P(None, "chan", None)),
        check_vma=False,
    )
```

profile of v0, /device:TPU:24, one launch (start us, length us, event | category | flops | bytes accessed | tf_op | source)
XLA Modules:
  0.0 384.9 jit_solution(320602423577932100)
XLA Ops:
  7.2 7.4 %collective-permute-start.1 = (bf16[1,32,2048]{2,1,0:T(8,128)(2,1)}, bf16[1,32,2048]{2,1,0:T(8,128)(2,1)S(1)}, u32[]{:S(2)}, u32[]{:S(2)}) collective-permute-start(bf16[1,32,2048]{2,1,0:T(8,128)(2,1)} %param.3), channel_id=1, source_target_pairs={{8,0},{16,8},{24,16},{32,24},{40,32},{48,40},{56,48},{64,56},{72,6... | collective-permute-start | bytes 393224 | tf_op jit(solution)/shard_map/ppermute | solution.py:18
  14.6 1.9 collective-permute-start
  16.6 1.5 slice_bitcast_fusion.54
  18.1 1.7 slice_bitcast_fusion.56
  19.8 1.0 reverse_bitcast_fusion
  22.3 0.9 collective-permute-done
  23.9 0.9 pad_maximum_fusion.1
  25.6 1.5 pad_slice_fusion.25
  27.1 2.8 pad_slice_fusion.26
  29.9 1.3 slice.794
  31.2 1.9 slice.785
  33.1 1.9 slice.787
  35.0 1.9 slice.796
  36.9 1.9 slice.726
  38.8 1.9 slice.792
  40.7 1.9 slice.728
  42.5 1.9 slice.730
  44.4 1.9 slice.735
  46.3 1.9 slice.737
  48.2 1.9 slice.739
  50.0 0.9 slice.744
  51.9 0.9 slice.748
  52.8 0.9 slice.753
  57.5 1.5 fusion.76
  63.5 1.8 fusion.45
  65.3 1.3 all-gather.2.cloned.1.call-done
  66.6 1.6 copy.7
  68.2 4.3 %collective-permute-start.3 = (bf16[1,256,2048]{1,2,0:T(8,128)(2,1)S(1)}, bf16[1,256,2048]{1,2,0:T(8,128)(2,1)S(1)}, u32[]{:S(2)}, u32[]{:S(2)}) collective-permute-start(bf16[1,256,2048]{1,2,0:T(8,128)(2,1)S(1)} %copy.7), channel_id=1, source_target_pairs={{8,0},{16,8},{24,16},{32,24},{40,32},{48,40},{56,48},{64,56},{72,6... | collective-permute-start | bytes 3145736 | tf_op jit(solution)/shard_map/ppermute | solution.py:18
  72.5 1.9 collective-permute-start.2
  74.4 1.9 fusion.73
  77.0 1.5 fusion.71
  79.1 1.5 fusion.69
  99.0 1.9 pad_maximum_fusion
  101.0 3.5 pad_slice_fusion.1
  104.5 8.9 %pad_slice_fusion.2 = (bf16[1,256,32,64]{1,3,2,0:T(8,128)(2,1)S(1)}, bf16[1,256,32,64]{1,3,2,0:T(8,128)(2,1)}, bf16[1,256,32,64]{1,3,2,0:T(8,128)(2,1)}, bf16[1,...) fusion(bf16[3,256,32,64]{1,3,2,0:T(8,128)(2,1)S(1)} %bitcast.398), kind=kLoop, calls=%fused_computation.94 | loop fusion | bytes 23068672 | tf_op jit(solution)/shard_map/slice | solution.py:35
  113.5 3.0 fusion
  116.7 1.0 fusion.25
  118.6 1.0 fusion.54
  120.4 1.0 fusion.53
  121.5 1.0 fusion.52
  122.7 2.3 fusion.51
  125.1 1.0 fusion.49
  126.6 1.0 fusion.48
  128.1 1.7 fusion.56
  129.8 22.9 %reduce-scatter.2.cloned.1.call-done = f32[1,32,2048]{2,1,0:T(8,128)} async-done(((f32[1,256,2048]{2,1,0:T(8,128)}), f32[1,32,2048]{2,1,0:T(8,128)}) %reduce-scatter.2.cloned.1.call-update) | async-done | bytes 262160 | tf_op jit(solution)/shard_map/reduce_scatter | solution.py:78
  152.7 1.6 convert_element_type.38
  154.4 221.8 %all-reduce.4.cloned.1.call-done = f32[27,32,256]{2,1,0:T(8,128)} async-done(((f32[27,32,256]{2,1,0:T(8,128)}), f32[27,32,256]{2,1,0:T(8,128)}) %all-reduce.4.cloned.1.call-update) | async-done | bytes 884752 | tf_op jit(solution)/shard_map/psum | solution.py:87
  376.2 2.2 copy.38
  (284 shorter events, 34.1 us)
Async XLA Ops:
  7.2 59.4 %all-gather.2.cloned.1.call-start = ((), (), s32[]{:S(2)}) async-start(), calls=%async_computation.2 | async-start | bytes 1179648 | tf_op jit(solution)/shard_map/all_gather | solution.py:81
  7.2 15.0 %collective-permute-start.1 = (bf16[1,32,2048]{2,1,0:T(8,128)(2,1)}, bf16[1,32,2048]{2,1,0:T(8,128)(2,1)S(1)}, u32[]{:S(2)}, u32[]{:S(2)}) collective-permute-start(bf16[1,32,2048]{2,1,0:T(8,128)(2,1)} %param.3), channel_id=1, source_target_pairs={{8,0},{16,8},{24,16},{32,24},{40,32},{48,40},{56,48},{64,56},{72,6... | collective-permute-start | bytes 393224 | tf_op jit(solution)/shard_map/ppermute | solution.py:18
  14.6 8.6 %collective-permute-start = (bf16[1,32,2048]{2,1,0:T(8,128)(2,1)}, bf16[1,32,2048]{2,1,0:T(8,128)(2,1)S(1)}, u32[]{:S(2)}, u32[]{:S(2)}) collective-permute-start(bf16[1,32,2048]{2,1,0:T(8,128)(2,1)} %param.3), channel_id=1, source_target_pairs={{0,8},{8,16},{16,24},{24,32},{32,40},{40,48},{48,56},{56,64},{64,7... | collective-permute-start | bytes 393224 | tf_op jit(solution)/shard_map/ppermute | solution.py:15
  16.6 136.2 %reduce-scatter.2.cloned.1.call-start = ((), (), s32[]{:S(2)}) async-start(), calls=%async_computation.1 | async-start | bytes 2359296 | tf_op jit(solution)/shard_map/reduce_scatter | solution.py:78
  29.9 20.1 %copy-start.11 = (bf16[1,32,32,64]{3,2,1,0:T(8,128)(2,1)S(1)}, bf16[1,32,32,64]{3,2,1,0:T(8,128)(2,1)}, u32[]{:S(2)}) copy-start(bf16[1,32,32,64]{3,2,1,0:T(8,128)(2,1)} %get-tuple-element.33) | copy-start | bytes 393220
  29.9 21.0 %copy-start.10 = (bf16[1,32,32,64]{3,2,1,0:T(8,128)(2,1)S(1)}, bf16[1,32,32,64]{3,2,1,0:T(8,128)(2,1)}, u32[]{:S(2)}) copy-start(bf16[1,32,32,64]{3,2,1,0:T(8,128)(2,1)} %get-tuple-element.34) | copy-start | bytes 393220
  29.9 22.0 %copy-start.9 = (bf16[1,32,32,64]{3,2,1,0:T(8,128)(2,1)S(1)}, bf16[1,32,32,64]{3,2,1,0:T(8,128)(2,1)}, u32[]{:S(2)}) copy-start(bf16[1,32,32,64]{3,2,1,0:T(8,128)(2,1)} %get-tuple-element.35) | copy-start | bytes 393220
  53.8 3.7 copy-start.35
  53.8 3.7 copy-start.40
  55.0 5.3 %copy-start.51 = (bf16[1,32,2048]{2,1,0:T(8,128)(2,1)}, bf16[1,32,2048]{2,1,0:T(8,128)(2,1)S(1)}, u32[]{:S(2)}) copy-start(bf16[1,32,2048]{2,1,0:T(8,128)(2,1)S(1)} %slice.757) | copy-start | bytes 393220
  55.2 3.8 copy-start.27
  55.5 3.5 copy-start.31
  55.8 3.3 copy-start.36
  56.1 5.7 %copy-start.29 = (bf16[1,32,2048]{2,1,0:T(8,128)(2,1)}, bf16[1,32,2048]{2,1,0:T(8,128)(2,1)S(1)}, u32[]{:S(2)}) copy-start(bf16[1,32,2048]{2,1,0:T(8,128)(2,1)S(1)} %slice.774) | copy-start | bytes 393220
  56.1 3.0 copy-start.41
  56.1 3.0 copy-start.45
  56.1 3.0 copy-start.49
  56.4 5.4 %copy-start.33 = (bf16[1,32,2048]{2,1,0:T(8,128)(2,1)}, bf16[1,32,2048]{2,1,0:T(8,128)(2,1)S(1)}, u32[]{:S(2)}) copy-start(bf16[1,32,2048]{2,1,0:T(8,128)(2,1)S(1)} %slice.776) | copy-start | bytes 393220
  56.7 5.1 %copy-start.38 = (bf16[1,32,2048]{2,1,0:T(8,128)(2,1)}, bf16[1,32,2048]{2,1,0:T(8,128)(2,1)S(1)}, u32[]{:S(2)}) copy-start(bf16[1,32,2048]{2,1,0:T(8,128)(2,1)S(1)} %slice.778) | copy-start | bytes 393220
  57.0 5.5 %copy-start.25 = (bf16[1,32,2048]{2,1,0:T(8,128)(2,1)}, bf16[1,32,2048]{2,1,0:T(8,128)(2,1)S(1)}, u32[]{:S(2)}) copy-start(bf16[1,32,2048]{2,1,0:T(8,128)(2,1)S(1)} %slice.783) | copy-start | bytes 393220
  65.2 310.9 %all-reduce.4.cloned.1.call-start = ((), (), s32[]{:S(2)}) async-start(), calls=%async_computation.3 | async-start | bytes 1769472 | tf_op jit(solution)/shard_map/psum | solution.py:87
  66.6 10.4 %copy-start.12 = (bf16[1,256,2048]{2,1,0:T(8,128)(2,1)S(1)}, bf16[1,256,2048]{2,1,0:T(8,128)(2,1)}, u32[]{:S(2)}) copy-start(bf16[1,256,2048]{2,1,0:T(8,128)(2,1)} %all-gather.2.cloned.1.call-done) | copy-start | bytes 3145732
  68.1 13.1 %copy-start.44 = (bf16[1,32,2048]{2,1,0:T(8,128)(2,1)S(1)}, bf16[1,32,2048]{2,1,0:T(8,128)(2,1)}, u32[]{:S(2)}) copy-start(bf16[1,32,2048]{2,1,0:T(8,128)(2,1)} %slice.753) | copy-start | bytes 393220
  68.2 13.1 %copy-start.48 = (bf16[1,32,2048]{2,1,0:T(8,128)(2,1)S(1)}, bf16[1,32,2048]{2,1,0:T(8,128)(2,1)}, u32[]{:S(2)}) copy-start(bf16[1,32,2048]{2,1,0:T(8,128)(2,1)} %slice.755) | copy-start | bytes 393220
  68.2 13.1 %copy-start.52 = (bf16[1,32,2048]{2,1,0:T(8,128)(2,1)S(1)}, bf16[1,32,2048]{2,1,0:T(8,128)(2,1)}, u32[]{:S(2)}) copy-start(bf16[1,32,2048]{2,1,0:T(8,128)(2,1)} %copy-done.51) | copy-start | bytes 393220
  68.2 30.8 %collective-permute-start.3 = (bf16[1,256,2048]{1,2,0:T(8,128)(2,1)S(1)}, bf16[1,256,2048]{1,2,0:T(8,128)(2,1)S(1)}, u32[]{:S(2)}, u32[]{:S(2)}) collective-permute-start(bf16[1,256,2048]{1,2,0:T(8,128)(2,1)S(1)} %copy.7), channel_id=1, source_target_pairs={{8,0},{16,8},{24,16},{32,24},{40,32},{48,40},{56,48},{64,56},{72,6... | collective-permute-start | bytes 3145736 | tf_op jit(solution)/shard_map/ppermute | solution.py:18
  72.5 26.5 %collective-permute-start.2 = (bf16[1,256,2048]{1,2,0:T(8,128)(2,1)S(1)}, bf16[1,256,2048]{1,2,0:T(8,128)(2,1)}, u32[]{:S(2)}, u32[]{:S(2)}) collective-permute-start(bf16[1,256,2048]{1,2,0:T(8,128)(2,1)S(1)} %copy.7), channel_id=1, source_target_pairs={{0,8},{8,16},{16,24},{24,32},{32,40},{40,48},{48,56},{56,64},{64,7... | collective-permute-start | bytes 3145736 | tf_op jit(solution)/shard_map/ppermute | solution.py:15
  76.3 6.1 %copy-start.54 = (bf16[1,32,2048]{2,1,0:T(8,128)(2,1)S(1)}, bf16[1,32,2048]{2,1,0:T(8,128)(2,1)}, u32[]{:S(2)}) copy-start(bf16[1,32,2048]{2,1,0:T(8,128)(2,1)} %param.3) | copy-start | bytes 393220
  76.3 6.1 %copy-start.57 = (bf16[1,32,2048]{2,1,0:T(8,128)(2,1)S(1)}, bf16[1,32,2048]{2,1,0:T(8,128)(2,1)}, u32[]{:S(2)}) copy-start(bf16[1,32,2048]{2,1,0:T(8,128)(2,1)} %copy-done.55) | copy-start | bytes 393220
  76.3 6.0 %copy-start.60 = (bf16[1,32,2048]{2,1,0:T(8,128)(2,1)S(1)}, bf16[1,32,2048]{2,1,0:T(8,128)(2,1)}, u32[]{:S(2)}) copy-start(bf16[1,32,2048]{2,1,0:T(8,128)(2,1)} %copy-done.58) | copy-start | bytes 393220
  78.5 5.0 %copy-start.28 = (bf16[1,32,2048]{2,1,0:T(8,128)(2,1)S(1)}, bf16[1,32,2048]{2,1,0:T(8,128)(2,1)}, u32[]{:S(2)}) copy-start(bf16[1,32,2048]{2,1,0:T(8,128)(2,1)} %copy-done.27) | copy-start | bytes 393220
  78.5 5.0 %copy-start.32 = (bf16[1,32,2048]{2,1,0:T(8,128)(2,1)S(1)}, bf16[1,32,2048]{2,1,0:T(8,128)(2,1)}, u32[]{:S(2)}) copy-start(bf16[1,32,2048]{2,1,0:T(8,128)(2,1)} %copy-done.31) | copy-start | bytes 393220
  78.5 5.0 %copy-start.37 = (bf16[1,32,2048]{2,1,0:T(8,128)(2,1)S(1)}, bf16[1,32,2048]{2,1,0:T(8,128)(2,1)}, u32[]{:S(2)}) copy-start(bf16[1,32,2048]{2,1,0:T(8,128)(2,1)} %copy-done.36) | copy-start | bytes 393220
  80.6 4.0 %copy-start.30 = (bf16[1,32,2048]{2,1,0:T(8,128)(2,1)S(1)}, bf16[1,32,2048]{2,1,0:T(8,128)(2,1)}, u32[]{:S(2)}) copy-start(bf16[1,32,2048]{2,1,0:T(8,128)(2,1)} %copy-done.29) | copy-start | bytes 393220
  80.6 4.0 %copy-start.34 = (bf16[1,32,2048]{2,1,0:T(8,128)(2,1)S(1)}, bf16[1,32,2048]{2,1,0:T(8,128)(2,1)}, u32[]{:S(2)}) copy-start(bf16[1,32,2048]{2,1,0:T(8,128)(2,1)} %copy-done.33) | copy-start | bytes 393220
  80.6 4.0 %copy-start.39 = (bf16[1,32,2048]{2,1,0:T(8,128)(2,1)S(1)}, bf16[1,32,2048]{2,1,0:T(8,128)(2,1)}, u32[]{:S(2)}) copy-start(bf16[1,32,2048]{2,1,0:T(8,128)(2,1)} %copy-done.38) | copy-start | bytes 393220
  81.7 3.9 %copy-start.24 = (bf16[1,32,2048]{2,1,0:T(8,128)(2,1)S(1)}, bf16[1,32,2048]{2,1,0:T(8,128)(2,1)}, u32[]{:S(2)}) copy-start(bf16[1,32,2048]{2,1,0:T(8,128)(2,1)} %slice.787) | copy-start | bytes 393220
  81.8 3.9 %copy-start.26 = (bf16[1,32,2048]{2,1,0:T(8,128)(2,1)S(1)}, bf16[1,32,2048]{2,1,0:T(8,128)(2,1)}, u32[]{:S(2)}) copy-start(bf16[1,32,2048]{2,1,0:T(8,128)(2,1)} %copy-done.25) | copy-start | bytes 393220
  82.9 3.9 %copy-start.22 = (bf16[1,32,2048]{2,1,0:T(8,128)(2,1)S(1)}, bf16[1,32,2048]{2,1,0:T(8,128)(2,1)}, u32[]{:S(2)}) copy-start(bf16[1,32,2048]{2,1,0:T(8,128)(2,1)} %slice.792) | copy-start | bytes 393220
  104.5 8.9 %copy-start.108 = (bf16[256,32]{0,1:T(8,128)(2,1)S(1)}, bf16[256,32]{0,1:T(8,128)(2,1)}, u32[]{:S(2)}) copy-start(bf16[256,32]{0,1:T(8,128)(2,1)} %get-tuple-element.75) | copy-start | bytes 49156
  104.5 8.9 %copy-start.109 = (bf16[256,32]{0,1:T(8,128)(2,1)S(1)}, bf16[256,32]{0,1:T(8,128)(2,1)}, u32[]{:S(2)}) copy-start(bf16[256,32]{0,1:T(8,128)(2,1)} %get-tuple-element.76) | copy-start | bytes 49156
  104.5 8.9 %copy-start.110 = (bf16[256,32]{0,1:T(8,128)(2,1)S(1)}, bf16[256,32]{0,1:T(8,128)(2,1)}, u32[]{:S(2)}) copy-start(bf16[256,32]{0,1:T(8,128)(2,1)} %get-tuple-element.77) | copy-start | bytes 49156
  113.4 3.1 copy-start.6
  113.4 3.1 copy-start.7
  113.4 3.1 copy-start.8
  113.5 3.1 copy-start.100
  113.5 3.1 copy-start.101
  113.5 3.1 copy-start.102
  (70 other events, 104.0 us)
Sparse Core Ops, SparseCore 0:
  16.7 49.8 all-gather.1
  70.6 82.0 reduce-scatter.1
  156.0 220.1 all-reduce.3
where the time goes:
time: 386 us; the launch traced here: 385 us
  waiting for transfers between devices  247 us (64%)
  local copies, waits for them, and re-layouts  75.3 us (20%)
  matrix products  27.3 us (7%)
  starting transfers between devices  15.7 us (4%)
  between operations  15.1 us (4%)
  other arithmetic  4.51 us (1%)
    psum x1, waiting for transfers between devices, local(): weight_grad = lax.psum(local_terms, 'space')  222 us
    slice x28, local copies, waits for them, and re-layouts, stack_at(): moved[tap_depth:tap_depth + planes]  43.6 us
    unnamed x249, local copies, waits for them, and re-layouts  23.1 us
    reduce_scatter x1, waiting for transfers between devices, local(): lax.psum_scatter(partial_out, 'chan', scatter_dimension=1, tiled=True)  22.9 us
    dot_general x18, matrix products, convolve(): jnp.einsum('dcp,co->dop', stack_at(padded, tap_row, tap_col), tap_weights...  19.7 us
    ppermute x2, starting transfers between devices, extended(): lax.ppermute(lax.slice_in_dim(block, 0, width, axis=dim), axis, backward)  11.7 us
  transfers between devices with their start and end apart: 7, of which 4 were waited for; matrix products, arithmetic and copies ran while one was open for 26% of the time, Pallas kernels for 0%

commit v1 on v0

--- a/solution.py
+++ b/solution.py
@@ -84,7 +84,7 @@
     flipped = jnp.transpose(weights[::-1], (0, 2, 1))
     input_grad = convolve(cot_padded, flipped).astype(jnp.bfloat16)
     local_terms = weight_terms(padded, cot_whole, inputs.shape[1])
-    weight_grad = lax.psum(local_terms, "space")
+    weight_grad = jnp.sum(lax.all_gather(local_terms, "space"), axis=0)
     return (output, input_grad, weight_grad)
 
 

time: 386 us -> 339 us (0.88)
  waiting for transfers between devices: 247 us -> 217 us
  local copies, waits for them, and re-layouts: 75.3 us -> 49.5 us
  other arithmetic: 4.51 us -> 14.4 us
    psum x1 -> x0, waiting for transfers between devices: 222 us -> none  [local(): weight_grad = lax.psum(local_terms, 'space')]
    all_gather x0 -> x1, waiting for transfers between devices: none -> 159 us  [local(): weight_grad = jnp.sum(lax.all_gather(local_terms, 'space'), axis=0)]
    unnamed x249 -> x182, local copies, waits for them, and re-layouts: 23.1 us -> 5.64 us
    reduce_sum x0 -> x1, other arithmetic: none -> 11.4 us  [local(): weight_grad = jnp.sum(lax.all_gather(local_terms, 'space'), axis=0)]
    reduce_scatter x1, waiting for transfers between devices: 22.9 us -> 34.1 us  [local(): lax.psum_scatter(partial_out, 'chan', scatter_dimension=1, tiled=True)]
    ppermute x2, waiting for transfers between devices: 0.01 us -> 10.3 us  [extended(): lax.ppermute(lax.slice_in_dim(block, 0, width, axis=dim), axis, backward)]
    ppermute x2, waiting for transfers between devices: 0.95 us -> 9.43 us  [extended(): lax.ppermute(lax.slice_in_dim(block, block.shape[dim] - width, None, axis...]
    slice x28, local copies, waits for them, and re-layouts: 43.6 us -> 39.4 us  [stack_at(): moved[tap_depth:tap_depth + planes]]
  transfers between devices with their start and end apart: 7 -> 7, of which waited for: 4 -> 6; matrix products, arithmetic and copies ran while one was open for 26% -> 22% of each run, Pallas kernels for 0% -> 0%
where the time goes in v1:
time: 339 us; the launch traced here: 336 us
  waiting for transfers between devices  217 us (64%)
  local copies, waits for them, and re-layouts  49.5 us (15%)
  matrix products  27.1 us (8%)
  between operations  15 us (4%)
  other arithmetic  14.4 us (4%)
  starting transfers between devices  13.8 us (4%)
    all_gather x1, waiting for transfers between devices, local(): weight_grad = jnp.sum(lax.all_gather(local_terms, 'space'), axis=0)  159 us
    slice x28, local copies, waits for them, and re-layouts, stack_at(): moved[tap_depth:tap_depth + planes]  39.4 us
    reduce_scatter x1, waiting for transfers between devices, local(): lax.psum_scatter(partial_out, 'chan', scatter_dimension=1, tiled=True)  34.1 us
    dot_general x18, matrix products, convolve(): jnp.einsum('dcp,co->dop', stack_at(padded, tap_row, tap_col), tap_weights...  18.3 us
    reduce_sum x1, other arithmetic, local(): weight_grad = jnp.sum(lax.all_gather(local_terms, 'space'), axis=0)  11.4 us
    ppermute x2, waiting for transfers between devices, extended(): lax.ppermute(lax.slice_in_dim(block, 0, width, axis=dim), axis, backward)  10.3 us
    ppermute x2, starting transfers between devices, extended(): lax.ppermute(lax.slice_in_dim(block, 0, width, axis=dim), axis, backward)  9.84 us
    ppermute x2, waiting for transfers between devices, extended(): lax.ppermute(lax.slice_in_dim(block, block.shape[dim] - width, None, axis...  9.43 us
  transfers between devices with their start and end apart: 7, of which 6 were waited for; matrix products, arithmetic and copies ran while one was open for 22% of the time, Pallas kernels for 0%

profile of v1, /device:TPU:24, one launch (start us, length us, event | category | flops | bytes accessed | tf_op | source)
XLA Modules:
  0.0 336.5 jit_solution(10008134416257139854)
XLA Ops:
  7.2 7.4 %collective-permute-start.1 = (bf16[1,32,2048]{2,1,0:T(8,128)(2,1)}, bf16[1,32,2048]{2,1,0:T(8,128)(2,1)S(1)}, u32[]{:S(2)}, u32[]{:S(2)}) collective-permute-start(bf16[1,32,2048]{2,1,0:T(8,128)(2,1)} %param.3), channel_id=1, source_target_pairs={{8,0},{16,8},{24,16},{32,24},{40,32},{48,40},{56,48},{64,56},{72,6... | collective-permute-start | bytes 393224 | tf_op jit(solution)/shard_map/ppermute | solution.py:18
  14.6 1.9 collective-permute-start
  16.6 1.6 slice_bitcast_fusion.56
  18.3 1.5 slice_bitcast_fusion.54
  19.8 3.4 %collective-permute-done = bf16[1,32,2048]{2,1,0:T(8,128)(2,1)S(1)} collective-permute-done((bf16[1,32,2048]{2,1,0:T(8,128)(2,1)}, bf16[1,32,2048]{2,1,0:T(8,128)(2,1)S(1)}, u32[]{:S(2)}, u32[]{:S(2)}) %collective-permute-start) | collective-permute-done | bytes 131104 | tf_op jit(solution)/shard_map/ppermute | solution.py:15
  23.9 0.9 pad_maximum_fusion.1
  25.6 2.8 pad_slice_fusion.26
  28.4 1.5 pad_slice_fusion.25
  29.9 1.3 slice.769
  31.2 1.9 slice.767
  33.1 1.9 slice.765
  35.0 1.9 slice.730
  36.8 1.9 slice.728
  38.7 1.9 slice.726
  40.6 1.9 slice.739
  42.5 1.9 slice.737
  44.4 0.9 slice.735
  46.2 0.9 slice.746
  47.1 0.9 slice.744
  48.1 0.9 slice.757
  49.0 0.9 slice.755
  51.7 1.3 slice.787
  55.0 1.5 fusion.76
  60.7 1.8 fusion.45
  62.5 4.1 %all-gather.4.cloned.1.call-done = bf16[1,256,2048]{2,1,0:T(8,128)(2,1)} async-done(((bf16[1,32,2048]{2,1,0:T(8,128)(2,1)}), bf16[1,256,2048]{2,1,0:T(8,128)(2,1)}) %all-gather.4.cloned.1.call-update) | async-done | bytes 1048592 | tf_op jit(solution)/shard_map/all_gather | solution.py:81
  66.6 1.8 fusion.73
  68.4 1.9 fusion.71
  70.3 1.4 fusion.69
  71.8 1.5 fusion.67
  77.5 2.4 collective-permute-start.3
  80.0 1.9 collective-permute-start.2
  82.0 10.3 %collective-permute-done.3 = bf16[1,256,2048]{1,2,0:T(8,128)(2,1)S(1)} collective-permute-done((bf16[1,256,2048]{1,2,0:T(8,128)(2,1)S(1)}, bf16[1,256,2048]{1,2,0:T(8,128)(2,1)S(1)}, u32[]{:S(2)}, u32[]{:S(2)}) %collective-permute-start.3) | collective-permute-done | bytes 1048608 | tf_op jit(solution)/shard_map/ppermute | solution.py:18
  92.3 6.0 %collective-permute-done.2 = bf16[1,256,2048]{1,2,0:T(8,128)(2,1)S(1)} collective-permute-done((bf16[1,256,2048]{1,2,0:T(8,128)(2,1)S(1)}, bf16[1,256,2048]{1,2,0:T(8,128)(2,1)S(1)}, u32[]{:S(2)}, u32[]{:S(2)}) %collective-permute-start.2) | collective-permute-done | bytes 1048608 | tf_op jit(solution)/shard_map/ppermute | solution.py:15
  99.3 8.9 %pad_slice_fusion.2 = (bf16[1,256,32,64]{1,3,2,0:T(8,128)(2,1)S(1)}, bf16[1,256,32,64]{1,3,2,0:T(8,128)(2,1)}, bf16[1,256,32,64]{1,3,2,0:T(8,128)(2,1)}, bf16[1,...) fusion(bf16[3,256,32,64]{1,3,2,0:T(8,128)(2,1)S(1)} %bitcast.399), kind=kLoop, calls=%fused_computation.94 | loop fusion | bytes 23068672 | tf_op jit(solution)/shard_map/slice | solution.py:35
  108.2 2.9 fusion.25
  111.2 1.8 pad_slice_fusion.1
  113.0 1.0 fusion
  114.9 1.0 fusion.54
  116.8 1.0 fusion.53
  117.8 1.0 fusion.52
  119.4 1.0 fusion.51
  120.4 1.0 fusion.49
  121.4 1.0 fusion.48
  122.4 1.7 fusion.56
  124.1 34.1 %reduce-scatter.2.cloned.1.call-done = f32[1,32,2048]{2,1,0:T(8,128)} async-done(((f32[1,256,2048]{2,1,0:T(8,128)}), f32[1,32,2048]{2,1,0:T(8,128)}) %reduce-scatter.2.cloned.1.call-update) | async-done | bytes 262160 | tf_op jit(solution)/shard_map/reduce_scatter | solution.py:78
  158.2 1.6 convert_element_type.38
  159.8 158.7 %all-gather.6.cloned.1.call-done = f32[864,32,256]{2,1,0:T(8,128)} async-done(((f32[27,32,256]{2,1,0:T(8,128)}), f32[864,32,256]{2,1,0:T(8,128)}) %all-gather.6.cloned.1.call-update) | async-done | bytes 28311568 | tf_op jit(solution)/shard_map/all_gather | solution.py:87
  318.5 11.4 %reduce_sum.9 = f32[27,32,256]{2,1,0:T(8,128)} reduce(f32[32,27,32,256]{3,2,1,0:T(8,128)} %bitcast.398, f32[]{:T(128)} %constant.4.clone.1), dimensions={0}, to_apply=%region_1.2 | reduce | flops 6856704 | bytes 29196292 | tf_op jit(solution)/shard_map/reduce_sum | solution.py:87
  (218 shorter events, 17.2 us)
Async XLA Ops:
  7.2 59.4 %all-gather.4.cloned.1.call-start = ((), (), s32[]{:S(2)}) async-start(), calls=%async_computation.2 | async-start | bytes 1179648 | tf_op jit(solution)/shard_map/all_gather | solution.py:81
  7.2 12.6 %collective-permute-start.1 = (bf16[1,32,2048]{2,1,0:T(8,128)(2,1)}, bf16[1,32,2048]{2,1,0:T(8,128)(2,1)S(1)}, u32[]{:S(2)}, u32[]{:S(2)}) collective-permute-start(bf16[1,32,2048]{2,1,0:T(8,128)(2,1)} %param.3), channel_id=1, source_target_pairs={{8,0},{16,8},{24,16},{32,24},{40,32},{48,40},{56,48},{64,56},{72,6... | collective-permute-start | bytes 393224 | tf_op jit(solution)/shard_map/ppermute | solution.py:18
  14.6 8.6 %collective-permute-start = (bf16[1,32,2048]{2,1,0:T(8,128)(2,1)}, bf16[1,32,2048]{2,1,0:T(8,128)(2,1)S(1)}, u32[]{:S(2)}, u32[]{:S(2)}) collective-permute-start(bf16[1,32,2048]{2,1,0:T(8,128)(2,1)} %param.3), channel_id=1, source_target_pairs={{0,8},{8,16},{16,24},{24,32},{32,40},{40,48},{48,56},{56,64},{64,7... | collective-permute-start | bytes 393224 | tf_op jit(solution)/shard_map/ppermute | solution.py:15
  16.6 141.6 %reduce-scatter.2.cloned.1.call-start = ((), (), s32[]{:S(2)}) async-start(), calls=%async_computation.1 | async-start | bytes 2359296 | tf_op jit(solution)/shard_map/reduce_scatter | solution.py:78
  19.8 3.4 %copy-start.49 = (bf16[1,32,2048]{2,1,0:T(8,128)(2,1)}, bf16[1,32,2048]{2,1,0:T(8,128)(2,1)S(1)}, u32[]{:S(2)}) copy-start(bf16[1,32,2048]{2,1,0:T(8,128)(2,1)S(1)} %collective-permute-done.1) | copy-start | bytes 393220
  29.9 14.5 %copy-start.10 = (bf16[1,32,32,64]{3,2,1,0:T(8,128)(2,1)S(1)}, bf16[1,32,32,64]{3,2,1,0:T(8,128)(2,1)}, u32[]{:S(2)}) copy-start(bf16[1,32,32,64]{3,2,1,0:T(8,128)(2,1)} %get-tuple-element.30) | copy-start | bytes 393220
  29.9 15.4 %copy-start.9 = (bf16[1,32,32,64]{3,2,1,0:T(8,128)(2,1)S(1)}, bf16[1,32,32,64]{3,2,1,0:T(8,128)(2,1)}, u32[]{:S(2)}) copy-start(bf16[1,32,32,64]{3,2,1,0:T(8,128)(2,1)} %get-tuple-element.35) | copy-start | bytes 393220
  40.6 13.3 %copy-start.16 = (bf16[1,32,32,64]{3,2,1,0:T(8,128)(2,1)S(1)}, bf16[1,32,32,64]{3,2,1,0:T(8,128)(2,1)}, u32[]{:S(2)}) copy-start(bf16[1,32,32,64]{3,2,1,0:T(8,128)(2,1)} %get-tuple-element.46) | copy-start | bytes 393220
  45.3 8.3 %copy-start.17 = (bf16[1,32,32,64]{3,2,1,0:T(8,128)(2,1)S(1)}, bf16[1,32,32,64]{3,2,1,0:T(8,128)(2,1)}, u32[]{:S(2)}) copy-start(bf16[1,32,32,64]{3,2,1,0:T(8,128)(2,1)} %get-tuple-element.49) | copy-start | bytes 393220
  46.2 6.7 %copy-start.18 = (bf16[1,32,32,64]{3,2,1,0:T(8,128)(2,1)S(1)}, bf16[1,32,32,64]{3,2,1,0:T(8,128)(2,1)}, u32[]{:S(2)}) copy-start(bf16[1,32,32,64]{3,2,1,0:T(8,128)(2,1)} %get-tuple-element.47) | copy-start | bytes 393220
  47.1 7.3 %copy-start.20 = (bf16[1,32,2048]{2,1,0:T(8,128)(2,1)S(1)}, bf16[1,32,2048]{2,1,0:T(8,128)(2,1)}, u32[]{:S(2)}) copy-start(bf16[1,32,2048]{2,1,0:T(8,128)(2,1)} %slice.767) | copy-start | bytes 393220
  47.1 7.3 %copy-start.21 = (bf16[1,32,2048]{2,1,0:T(8,128)(2,1)S(1)}, bf16[1,32,2048]{2,1,0:T(8,128)(2,1)}, u32[]{:S(2)}) copy-start(bf16[1,32,2048]{2,1,0:T(8,128)(2,1)} %slice.765) | copy-start | bytes 393220
  48.1 6.4 %copy-start.71 = (bf16[32,256]{1,0:T(8,128)(2,1)S(1)}, bf16[32,256]{1,0:T(8,128)(2,1)}, u32[]{:S(2)}) copy-start(bf16[32,256]{1,0:T(8,128)(2,1)} %get-tuple-element.86) | copy-start | bytes 49156
  48.1 6.4 %copy-start.72 = (bf16[32,256]{1,0:T(8,128)(2,1)S(1)}, bf16[32,256]{1,0:T(8,128)(2,1)}, u32[]{:S(2)}) copy-start(bf16[32,256]{1,0:T(8,128)(2,1)} %get-tuple-element.87) | copy-start | bytes 49156
  48.1 6.4 %copy-start.73 = (bf16[32,256]{1,0:T(8,128)(2,1)S(1)}, bf16[32,256]{1,0:T(8,128)(2,1)}, u32[]{:S(2)}) copy-start(bf16[32,256]{1,0:T(8,128)(2,1)} %get-tuple-element.88) | copy-start | bytes 49156
  50.9 4.1 %copy-start.30 = (bf16[1,32,2048]{2,1,0:T(8,128)(2,1)S(1)}, bf16[1,32,2048]{2,1,0:T(8,128)(2,1)}, u32[]{:S(2)}) copy-start(bf16[1,32,2048]{2,1,0:T(8,128)(2,1)} %slice.730) | copy-start | bytes 393220
  50.9 4.1 %copy-start.32 = (bf16[1,32,2048]{2,1,0:T(8,128)(2,1)S(1)}, bf16[1,32,2048]{2,1,0:T(8,128)(2,1)}, u32[]{:S(2)}) copy-start(bf16[1,32,2048]{2,1,0:T(8,128)(2,1)} %slice.728) | copy-start | bytes 393220
  51.7 7.5 %copy-start.22 = (bf16[1,32,2048]{2,1,0:T(8,128)(2,1)}, bf16[1,32,2048]{2,1,0:T(8,128)(2,1)S(1)}, u32[]{:S(2)}) copy-start(bf16[1,32,2048]{2,1,0:T(8,128)(2,1)S(1)} %slice.774) | copy-start | bytes 393220
  53.5 6.4 %copy-start.24 = (bf16[1,32,2048]{2,1,0:T(8,128)(2,1)}, bf16[1,32,2048]{2,1,0:T(8,128)(2,1)S(1)}, u32[]{:S(2)}) copy-start(bf16[1,32,2048]{2,1,0:T(8,128)(2,1)S(1)} %slice.783) | copy-start | bytes 393220
  53.5 3.0 copy-start.34
  53.5 3.0 copy-start.41
  53.5 3.0 copy-start.44
  53.6 3.0 copy-start.75
  53.6 3.0 copy-start.76
  53.6 3.0 copy-start.77
  54.1 6.4 %copy-start.26 = (bf16[1,32,2048]{2,1,0:T(8,128)(2,1)}, bf16[1,32,2048]{2,1,0:T(8,128)(2,1)S(1)}, u32[]{:S(2)}) copy-start(bf16[1,32,2048]{2,1,0:T(8,128)(2,1)S(1)} %slice.794) | copy-start | bytes 393220
  54.4 6.2 %copy-start.28 = (bf16[1,32,2048]{2,1,0:T(8,128)(2,1)}, bf16[1,32,2048]{2,1,0:T(8,128)(2,1)S(1)}, u32[]{:S(2)}) copy-start(bf16[1,32,2048]{2,1,0:T(8,128)(2,1)S(1)} %slice.792) | copy-start | bytes 393220
  54.9 2.1 copy-start.36
  55.0 2.1 copy-start.42
  55.0 2.1 copy-start.45
  55.0 2.1 copy-start.69
  55.0 2.1 copy-start.70
  60.6 6.0 %copy-start.31 = (bf16[1,32,2048]{2,1,0:T(8,128)(2,1)S(1)}, bf16[1,32,2048]{2,1,0:T(8,128)(2,1)}, u32[]{:S(2)}) copy-start(bf16[1,32,2048]{2,1,0:T(8,128)(2,1)} %slice.730) | copy-start | bytes 393220
  60.6 6.0 %copy-start.33 = (bf16[1,32,2048]{2,1,0:T(8,128)(2,1)S(1)}, bf16[1,32,2048]{2,1,0:T(8,128)(2,1)}, u32[]{:S(2)}) copy-start(bf16[1,32,2048]{2,1,0:T(8,128)(2,1)} %slice.728) | copy-start | bytes 393220
  60.6 5.9 %copy-start.40 = (bf16[1,32,2048]{2,1,0:T(8,128)(2,1)S(1)}, bf16[1,32,2048]{2,1,0:T(8,128)(2,1)}, u32[]{:S(2)}) copy-start(bf16[1,32,2048]{2,1,0:T(8,128)(2,1)} %slice.726) | copy-start | bytes 393220
  62.4 6.0 %copy-start.35 = (bf16[1,32,2048]{2,1,0:T(8,128)(2,1)S(1)}, bf16[1,32,2048]{2,1,0:T(8,128)(2,1)}, u32[]{:S(2)}) copy-start(bf16[1,32,2048]{2,1,0:T(8,128)(2,1)} %slice.739) | copy-start | bytes 393220
  62.4 7.9 %copy-start.37 = (bf16[1,32,2048]{2,1,0:T(8,128)(2,1)S(1)}, bf16[1,32,2048]{2,1,0:T(8,128)(2,1)}, u32[]{:S(2)}) copy-start(bf16[1,32,2048]{2,1,0:T(8,128)(2,1)} %slice.748) | copy-start | bytes 393220
  62.4 9.4 %copy-start.39 = (bf16[1,32,2048]{2,1,0:T(8,128)(2,1)S(1)}, bf16[1,32,2048]{2,1,0:T(8,128)(2,1)}, u32[]{:S(2)}) copy-start(bf16[1,32,2048]{2,1,0:T(8,128)(2,1)} %slice.757) | copy-start | bytes 393220
  62.5 256.1 %all-gather.6.cloned.1.call-start = ((), (), s32[]{:S(2)}) async-start(), calls=%async_computation.3 | async-start | bytes 29196288 | tf_op jit(solution)/shard_map/all_gather | solution.py:87
  66.6 3.8 %copy-start.11 = (bf16[1,256,2048]{2,1,0:T(8,128)(2,1)S(1)}, bf16[1,256,2048]{2,1,0:T(8,128)(2,1)}, u32[]{:S(2)}) copy-start(bf16[1,256,2048]{2,1,0:T(8,128)(2,1)} %all-gather.4.cloned.1.call-done) | copy-start | bytes 3145732
  68.4 4.9 %copy-start.48 = (bf16[1,32,2048]{2,1,0:T(8,128)(2,1)S(1)}, bf16[1,32,2048]{2,1,0:T(8,128)(2,1)}, u32[]{:S(2)}) copy-start(bf16[1,32,2048]{2,1,0:T(8,128)(2,1)} %param.3) | copy-start | bytes 393220
  68.4 4.9 %copy-start.51 = (bf16[1,32,2048]{2,1,0:T(8,128)(2,1)S(1)}, bf16[1,32,2048]{2,1,0:T(8,128)(2,1)}, u32[]{:S(2)}) copy-start(bf16[1,32,2048]{2,1,0:T(8,128)(2,1)} %copy-done.49) | copy-start | bytes 393220
  68.4 4.9 %copy-start.54 = (bf16[1,32,2048]{2,1,0:T(8,128)(2,1)S(1)}, bf16[1,32,2048]{2,1,0:T(8,128)(2,1)}, u32[]{:S(2)}) copy-start(bf16[1,32,2048]{2,1,0:T(8,128)(2,1)} %copy-done.52) | copy-start | bytes 393220
  71.8 2.5 copy-start.23
  75.3 6.6 %copy-start = (bf16[27,32,256]{2,1,0:T(8,128)(2,1)S(1)}, bf16[27,32,256]{2,1,0:T(8,128)(2,1)}, u32[]{:S(2)}) copy-start(bf16[27,32,256]{2,1,0:T(8,128)(2,1)} %param.4) | copy-start | bytes 1327108
  77.5 14.8 %collective-permute-start.3 = (bf16[1,256,2048]{1,2,0:T(8,128)(2,1)S(1)}, bf16[1,256,2048]{1,2,0:T(8,128)(2,1)S(1)}, u32[]{:S(2)}, u32[]{:S(2)}) collective-permute-start(bf16[1,256,2048]{1,2,0:T(8,128)(2,1)S(1)} %copy.7), channel_id=1, source_target_pairs={{8,0},{16,8},{24,16},{32,24},{40,32},{48,40},{56,48},{64,56},{72,6... | collective-permute-start | bytes 3145736 | tf_op jit(solution)/shard_map/ppermute | solution.py:18
  80.0 18.3 %collective-permute-start.2 = (bf16[1,256,2048]{1,2,0:T(8,128)(2,1)S(1)}, bf16[1,256,2048]{1,2,0:T(8,128)(2,1)S(1)}, u32[]{:S(2)}, u32[]{:S(2)}) collective-permute-start(bf16[1,256,2048]{1,2,0:T(8,128)(2,1)S(1)} %copy.7), channel_id=1, source_target_pairs={{0,8},{8,16},{16,24},{24,32},{32,40},{40,48},{48,56},{56,64},{64,7... | collective-permute-start | bytes 3145736 | tf_op jit(solution)/shard_map/ppermute | solution.py:15
  92.3 6.3 %copy-start.12 = (bf16[1,256,2048]{1,2,0:T(8,128)(2,1)}, bf16[1,256,2048]{1,2,0:T(8,128)(2,1)S(1)}, u32[]{:S(2)}) copy-start(bf16[1,256,2048]{1,2,0:T(8,128)(2,1)S(1)} %collective-permute-done.3) | copy-start | bytes 3145732
  (37 other events, 42.9 us)
Sparse Core Ops, SparseCore 0:
  16.7 49.8 all-gather.3
  70.6 87.5 reduce-scatter.1
  160.6 157.8 all-gather.5
